TPU v7x, 256 devices: a whole 4x4x8 slice. The times are simulated.
256 devices in a mesh: gx: 8 (over x, core), gy: 32 (over y, z).
Axes of the slice: x: 4, y: 4, z: 8, core: 2. Of those that a mesh axis runs over, the one named last changes fastest.
Arguments:
- hidden_in: bfloat16 [8192, 4096], P('gx', 'gy')
- norm_gain: bfloat16 [4096], P('gy'), may hold values from 0.099609375 to 1.8984375
- query_proj: bfloat16 [4096, 4096], P('gx', 'gy')
- kv_proj: bfloat16 [1024, 4096], P(None, 'gy')
- prompt_lengths: int32 [8], replicated, may hold values from 1 to 4096, 8192 in all
- cache_slot: int32 [512], replicated, may hold values from 0 to 511, as said below
Outputs:
- attention: bfloat16 [8192, 4096], P('gy', 'gx')
- kv_cache: bfloat16 [512, 16, 1024], P('gy', None, 'gx')
Inputs may be any that keep to these rules, and one draw needn't show every extreme that they name: `prompt_lengths`: the 8 prompts sum to 8192 tokens; the longest has exactly 4096. `cache_slot`: A permutation of the 512 slots; slot s is held by index s // 16 of gy. The 16 pages of one token block go to any one index at most 1 times, and every index receives exactly 16 pages.
All inputs are finite; a program needn't handle non-finite values.
Results may differ from a plain program's by a relative error of at most 0.0066.
The roundings to bfloat16 on the way count: a program that leaves them out, or rounds other values in their place, can miss the bound.
Values may be sent and summed in bfloat16 or wider, within the bound.
No kernel may reach another device: no remote copies, remote signals or barrier semaphores. Data moves between devices by JAX's collectives and lax.ppermute only.
A program may use at most 128 MiB of HBM per device.

v0:
```python
import math
import jax
import jax.numpy as jnp
from jax import lax
from jax.sharding import PartitionSpec as P

D = 4096
H = 32
KVH = 4
HD = 128
PAGES_DEV = 16
MOST = 4096
epsilon = 1e-06
rope_base = 5000000.0
masked_out = -1e30


def token_places(prompt_lengths, token_index):
    prompt_ends = jnp.cumsum(prompt_lengths)
    prompt_starts = prompt_ends - prompt_lengths
    segment = jnp.sum((token_index[:, None] >= prompt_ends[None, :]).astype(jnp.int32), axis=1)
    chosen = segment[:, None] == jnp.arange(prompt_lengths.shape[0], dtype=jnp.int32)[None, :]
    opening = jnp.sum(jnp.where(chosen, prompt_starts[None, :], 0), axis=1)
    return (segment, token_index - opening)


def rotate(vectors, places):
    half_size = vectors.shape[-1] // 2
    frequency = rope_base ** (-(jnp.arange(half_size, dtype=jnp.float32) * 2.0) / vectors.shape[-1])
    angles = places.astype(jnp.float32)[:, None] * frequency[None, :]
    cos_part = jnp.cos(angles)[:, None, :]
    sin_part = jnp.sin(angles)[:, None, :]
    leading = vectors[..., :half_size]
    trailing = vectors[..., half_size:]
    return jnp.concatenate(
        [leading * cos_part - trailing * sin_part, trailing * cos_part + leading * sin_part],
        axis=-1,
    )


def local(hidden_in, norm_gain, query_proj, kv_proj, prompt_lengths, cache_slot):
    count_gx = lax.axis_size("gx")
    count_gy = lax.axis_size("gy")
    where_gx = lax.axis_index("gx")
    where_gy = lax.axis_index("gy")
    local_rows, local_feats = hidden_in.shape
    features = local_feats * count_gy
    block_tokens = local_rows * count_gx // count_gy
    all_tokens = block_tokens * count_gy
    blocks_per_slab = local_rows // block_tokens
    sub = block_tokens // count_gy
    heads_here = query_proj.shape[0] // HD
    query_cols = heads_here * HD
    is_key = where_gx % 2 == 0
    kv_rows = lax.dynamic_slice_in_dim(kv_proj, where_gx * HD, HD, 0)
    stacked = jnp.concatenate([query_proj, kv_rows], axis=0)
    weights_full = lax.all_gather(stacked, "gy", axis=1, tiled=True)
    gain_full = lax.all_gather(norm_gain, "gy", axis=0, tiled=True)
    pieces = hidden_in.reshape(blocks_per_slab, count_gy, sub, local_feats)
    pieces = lax.all_to_all(pieces, "gy", 1, 1, tiled=True)
    rows_here = lax.all_gather(pieces, "gx", axis=0, tiled=False)
    rows_here = rows_here.transpose(0, 1, 3, 2, 4).reshape(block_tokens, features)
    widened = rows_here.astype(jnp.float32)
    squares = jnp.sum(widened * widened, axis=1)
    normed = (
        widened
        * lax.rsqrt(squares / features + epsilon)[:, None]
        * gain_full.astype(jnp.float32)[None, :]
    ).astype(jnp.bfloat16)
    contract = (((1,), (1,)), ((), ()))
    projected = lax.dot_general(normed, weights_full, contract, preferred_element_type=jnp.float32)
    order = jnp.arange(block_tokens, dtype=jnp.int32)
    my_tokens = order // sub * block_tokens + where_gy * sub + order % sub
    unused_segment, my_places = token_places(prompt_lengths, my_tokens)
    queries = rotate(
        projected[:, :query_cols].reshape(block_tokens, heads_here, HD), my_places
    ).astype(jnp.bfloat16)
    half_raw = projected[:, query_cols:]
    rotated = rotate(half_raw[:, None, :], my_places)[:, 0, :]
    mine = jnp.where(is_key, rotated, half_raw).astype(jnp.bfloat16)
    queries = lax.all_to_all(
        queries.reshape(count_gy, sub, query_cols), "gy", 0, 0, tiled=True
    ).reshape(block_tokens, heads_here, HD)
    mine_all = lax.all_gather(mine.reshape(count_gy, sub, HD), "gy", axis=0, tiled=False)
    mine_all = mine_all.transpose(1, 0, 2, 3).reshape(all_tokens, HD)
    other_all = lax.ppermute(mine_all, "gx", [(p, p ^ 1) for p in range(count_gx)])
    keys = jnp.where(is_key, mine_all, other_all)
    values = jnp.where(is_key, other_all, mine_all)
    every_index = jnp.arange(all_tokens, dtype=jnp.int32)
    segment_all, unused_places = token_places(prompt_lengths, every_index)
    first_query = where_gy * block_tokens
    token_index = first_query + order
    segment_own = lax.dynamic_slice_in_dim(segment_all, first_query, block_tokens, 0)
    window_blocks = min(count_gy, MOST // block_tokens + 1)
    window = window_blocks * block_tokens
    window_start = (
        jnp.clip(where_gy - (window_blocks - 1), 0, count_gy - window_blocks) * block_tokens
    )
    key_rows = lax.dynamic_slice_in_dim(keys, window_start, window, 0)
    value_rows = lax.dynamic_slice_in_dim(values, window_start, window, 0)
    key_segment = lax.dynamic_slice_in_dim(segment_all, window_start, window, 0)
    key_index = window_start + jnp.arange(window, dtype=jnp.int32)
    allowed = (key_segment[None, :] == segment_own[:, None]) & (
        key_index[None, :] <= token_index[:, None]
    )
    score_scale = 1.0 / math.sqrt(HD)
    scores = (
        jnp.einsum("qhd,kd->hqk", queries, key_rows, preferred_element_type=jnp.float32)
        * score_scale
    )
    scores = jnp.where(allowed[None], scores, masked_out)
    row_max = jnp.max(scores, axis=2, keepdims=True)
    weights = jnp.where(allowed[None], jnp.exp(scores - row_max), 0.0)
    totals = jnp.sum(weights, axis=2)
    mixed = jnp.einsum(
        "hqk,kd->hqd", weights.astype(jnp.bfloat16), value_rows, preferred_element_type=jnp.float32
    )
    attention = (
        (mixed / totals[..., None])
        .astype(jnp.bfloat16)
        .transpose(1, 0, 2)
        .reshape(block_tokens, query_cols)
    )
    cache_cols = lax.dynamic_slice_in_dim(mine_all, first_query, block_tokens, 0)
    pages_dev = PAGES_DEV
    page_len = block_tokens // pages_dev
    page_range = jnp.arange(pages_dev, dtype=jnp.int32)
    width_cols = cache_cols.shape[1]
    my_pages = cache_cols.reshape(pages_dev, page_len * width_cols)
    capacity = max(1, pages_dev // count_gy)
    slots_all = count_gy * capacity
    owners = (cache_slot // pages_dev).reshape(count_gy, pages_dev)
    earlier = page_range[None, :] < page_range[:, None]
    same_owner = owners[:, :, None] == owners[:, None, :]
    ranks = jnp.sum((same_owner & earlier[None]).astype(jnp.int32), axis=2)
    my_owner = lax.dynamic_index_in_dim(owners, where_gy, 0, keepdims=False)
    my_rank = lax.dynamic_index_in_dim(ranks, where_gy, 0, keepdims=False)
    target = my_owner * capacity + my_rank
    slot_range = jnp.arange(slots_all, dtype=jnp.int32)
    send_map = (slot_range[:, None] == target[None, :]).astype(jnp.bfloat16)
    outgoing = jnp.dot(send_map, my_pages, preferred_element_type=jnp.float32).astype(jnp.bfloat16)
    incoming = lax.all_to_all(outgoing, "gy", split_axis=0, concat_axis=0, tiled=True)
    wanted = where_gy * pages_dev + page_range
    matches = cache_slot[None, :] == wanted[:, None]
    page_ids = jnp.arange(cache_slot.shape[0], dtype=jnp.int32)
    source_page = jnp.sum(jnp.where(matches, page_ids[None, :], 0), axis=1)
    source_rank = jnp.sum(jnp.where(matches, ranks.reshape(-1)[None, :], 0), axis=1)
    source_slot = source_page // pages_dev * capacity + source_rank
    take_map = (source_slot[:, None] == slot_range[None, :]).astype(jnp.bfloat16)
    cache_block = jnp.dot(take_map, incoming, preferred_element_type=jnp.float32)
    cache_block = cache_block.astype(jnp.bfloat16).reshape(pages_dev, page_len, width_cols)
    return (attention, cache_block)


def solution(mesh):
    return jax.shard_map(
        local,
        mesh=mesh,
        in_specs=(P("gx", "gy"), P("gy"), P("gx", "gy"), P(None, "gy"), P(), P()),
        out_specs=(P("gy", "gx"), P("gy", None, "gx")),
        check_vma=False,
    )
```

profile of v0, /device:TPU:2, one launch (start us, length us, event | category | flops | bytes accessed | tf_op | source)
XLA Modules:
  0.0 317.1 jit_solution(16310074648877330027)
XLA Ops:
  7.2 1.0 copy.44
  8.3 23.7 %all_to_all.22 = bf16[4,32,8,128]{3,2,0,1:T(8,128)(2,1)S(1)} all-to-all(bf16[4,32,8,128]{3,2,0,1:T(8,128)(2,1)S(1)} %copy.44), channel_id=1, replica_groups=mesh['gx'=8,'gy'=32] {'gy'}, dimensions={1} | all-to-all | bytes 524288 | tf_op jit(solution)/shard_map/all_to_all | solution.py:60
  32.0 0.7 copy.45
  32.8 1.6 pad_maximum_fusion.1
  34.5 36.5 %all-gather.1 = bf16[32,1,128]{2,1,0:T(2,128)(2,1)S(1)} all-gather(bf16[1,1,128]{2,1,0:T(2,128)(2,1)} %bitcast.75), channel_id=1, replica_groups=mesh['gx'=8,'gy'=32] {'gy'}, dimensions={0}, use_global_device_ids=true | all-gather | bytes 8448 | tf_op jit(solution)/shard_map/all_gather | solution.py:58
  71.0 0.8 reduce-window.8
  71.9 0.7 bitcast_subtract_fusion
  72.7 2.1 multiply_reduce_fusion
  74.9 4.1 %bitcast_convert_fusion = f32[8,4,32,8,128]{4,3,2,1,0:T(8,128)} fusion(bf16[32,32,8,128]{3,2,1,0:T(8,128)(2,1)} %all-gather.10.cloned.1.call-done), kind=kLoop, calls=%fused_computation.103 | loop fusion | flops 1048576 | bytes 6291456 | tf_op jit(solution)/shard_map/convert_element_type | solution.py:63
  79.0 67.4 %all-gather.6.cloned.1.call-done = bf16[640,4096]{1,0:T(8,128)(2,1)} async-done(((bf16[640,128]{1,0:T(8,128)(2,1)}), bf16[640,4096]{1,0:T(8,128)(2,1)}) %all-gather.6.cloned.1.call-update) | async-done | bytes 5242896 | tf_op jit(solution)/shard_map/all_gather | solution.py:57
  146.4 5.6 %fusion.8 = f32[256,640]{1,0:T(8,128)S(1)} fusion(bf16[640,4096]{1,0:T(8,128)(2,1)} %all-gather.6.cloned.1.call-done, f32[256,4096]{1,0:T(8,128)} %bitcast.62, f32[4096]{0:T(1024)S(1)} %bitcast.71, f32[256]{0:T(256)S(1)} %rsqrt.11), kind=kOutput, calls=%fused_computation.15 | convolution fusion | flops 1345323008 | bytes 10109952 | tf_op jit(solution)/shard_map/dot_general | solution.py:71
  152.0 0.6 fusion.37
  152.6 0.7 fusion.43
  153.7 1.2 multiply_cosine_fusion
  154.9 77.7 %all-gather.8.cloned.1.call-done = bf16[32,32,8,128]{3,2,1,0:T(8,128)(2,1)} async-done(((bf16[1,32,8,128]{3,2,1,0:T(8,128)(2,1)}), bf16[32,32,8,128]{3,2,1,0:T(8,128)(2,1)}) %all-gather.8.cloned.1.call-update) | async-done | bytes 2097168 | tf_op jit(solution)/shard_map/all_gather | solution.py:84
  232.6 2.2 copy.46
  234.9 4.4 %compare_and_fusion = pred[256,4352]{0,1:T(8,128)(4,1)} fusion(s32[256]{0:T(256)S(1)} %iota_add_fusion.1, s32[256]{0:T(256)S(1)} %dynamic_slice.26, s32[4352]{0:T(1024)S(1)} %iota_add_fusion, s32[4352]{0:T(1024)S(1)} %dynamic_slice.25), kind=kLoop, calls=%fused_computation.9 | loop fusion | flops 3342336 | bytes 1150976 | tf_op jit(solution)/shard_map/and | solution.py:103
  239.5 1.4 subtract_convert_fusion
  241.3 0.8 convert_element_type.69
  242.1 5.6 %all-to-all-start.1 = ((bf16[32,8,512]{2,1,0:T(8,128)(2,1)}), bf16[32,8,512]{2,1,0:T(8,128)(2,1)S(1)}, u32[]{:S(2)}, u32[]{:S(2)}) async-start(bf16[32,8,512]{2,1,0:T(8,128)(2,1)} %convert_element_type.69), calls=%async_computation.1 | async-start | bytes 524288 | tf_op jit(solution)/shard_map/all_to_all | solution.py:81
  248.6 0.5 broadcast.313
  249.1 0.7 reduce.4
  249.8 0.7 reshape.327
  250.5 9.8 %all-to-all-done.1 = bf16[32,8,512]{2,1,0:T(8,128)(2,1)S(1)} async-done(((bf16[32,8,512]{2,1,0:T(8,128)(2,1)}), bf16[32,8,512]{2,1,0:T(8,128)(2,1)S(1)}, u32[]{:S(2)}, u32[]{:S(2)}) %all-to-all-start.1) | async-done | bytes 262176 | tf_op jit(solution)/shard_map/all_to_all | solution.py:81
  260.3 5.1 %all-to-all-start.2 = ((bf16[32,2,1024]{2,1,0:T(2,128)(2,1)}), bf16[32,2,1024]{2,1,0:T(2,128)(2,1)S(1)}, u32[]{:S(2)}, u32[]{:S(2)}) async-start(bf16[32,2,1024]{2,1,0:T(2,128)(2,1)} %reshape.327), calls=%async_computation.2 | async-start | bytes 262144 | tf_op jit(solution)/shard_map/all_to_all | solution.py:142
  265.6 0.8 reshape.313
  266.3 9.1 %all-to-all-done.2 = bf16[32,2,1024]{2,1,0:T(2,128)(2,1)S(1)} async-done(((bf16[32,2,1024]{2,1,0:T(2,128)(2,1)}), bf16[32,2,1024]{2,1,0:T(2,128)(2,1)S(1)}, u32[]{:S(2)}, u32[]{:S(2)}) %all-to-all-start.2) | async-done | bytes 131104 | tf_op jit(solution)/shard_map/all_to_all | solution.py:142
  275.8 0.6 copy.60
  276.4 10.0 %fusion.22 = f32[4352,256,4]{1,0,2:T(8,128)} fusion(pred[]{:T(512)S(6)} %eq.96, bf16[8192,128]{1,0:T(8,128)(2,1)} %collective-permute-done, s32[]{:T(128)S(6)} %select_n.101, bf16[8192,128]{1,0:T(8,128)(2,1)S(1)} %bitcast.66, bf16[256,4,128]{2,1,0:T(4,128)(2,1)} %reshape.313), kind=kOutput, calls=%fused_computation.23 | convolution fusion | flops 1141407744 | bytes 20316164 | tf_op jit(solution)/shard_map/qhd,kd->hqk/dot_general | solution.py:108
  286.4 18.1 %fusion.60 = (f32[4,256]{1,0:T(4,128)S(1)}, bf16[4,256,4352]{1,2,0:T(8,128)(2,1)}) fusion(f32[4352,256,4]{1,0,2:T(8,128)} %fusion.22, pred[256,4352]{0,1:T(8,128)(4,1)S(1)} %copy-done.1), kind=kOutput, calls=%fused_computation.107 | output fusion | flops 35655936 | bytes 27856896 | tf_op jit(solution)/shard_map/sub | solution.py:113
  304.5 5.3 %fusion.17 = bf16[256,4,128]{0,2,1:T(8,128)(2,1)S(1)} fusion(bf16[4,256,4352]{1,2,0:T(8,128)(2,1)} %get-tuple-element.23, pred[]{:T(512)S(6)} %eq.96, bf16[8192,128]{1,0:T(8,128)(2,1)} %collective-permute-done, s32[]{:T(128)S(6)} %select_n.101, bf16[8192,128]{1,0:T(8,128)(2,1)S(1)} %bitcast.67, f32[256,4]{0,1:T(4,128)S(1)} %bitcast.77), kind=kOutput, calls=%fused_computation.20 | convolution fusion | flops 1141669888 | bytes 11407365 | tf_op jit(solution)/shard_map/hqk,kd->hqd/dot_general | solution.py:115
  309.8 0.8 copy.55
  (49 shorter events, 2.9 us)
Async XLA Ops:
  7.2 25.7 %copy-start = (bf16[1024,128]{1,0:T(8,128)(2,1)S(1)}, bf16[1024,128]{1,0:T(8,128)(2,1)}, u32[]{:S(2)}) copy-start(bf16[1024,128]{1,0:T(8,128)(2,1)} %param.9) | copy-start | bytes 786436
  7.2 65.5 %all-gather.10.cloned.1.call-start = ((), (), s32[]{:S(2)}) async-start(), calls=%async_computation.5 | async-start | bytes 2359296 | tf_op jit(solution)/shard_map/all_gather | solution.py:61
  32.8 113.6 %all-gather.6.cloned.1.call-start = ((), (), s32[]{:S(2)}) async-start(), calls=%async_computation.3 | async-start | bytes 5406720 | tf_op jit(solution)/shard_map/all_gather | solution.py:57
  34.4 198.2 %all-gather.8.cloned.1.call-start = ((), (), s32[]{:S(2)}) async-start(), calls=%async_computation.4 | async-start | bytes 2162688 | tf_op jit(solution)/shard_map/all_gather | solution.py:84
  146.4 7.3 %copy-start.2 = (s32[512]{0:T(512)S(1)}, s32[512]{0:T(512)}, u32[]{:S(2)}) copy-start(s32[512]{0:T(512)} %param.11) | copy-start | bytes 6148
  234.8 41.6 %collective-permute-start = (bf16[8192,128]{1,0:T(8,128)(2,1)S(1)}, bf16[8192,128]{1,0:T(8,128)(2,1)}, u32[]{:S(2)}, u32[]{:S(2)}) collective-permute-start(bf16[8192,128]{1,0:T(8,128)(2,1)S(1)} %bitcast.64), channel_id=1, source_target_pairs={{0,32},{32,0},{64,96},{96,64},{128,160},{160,128},{192,224},{224,1... | collective-permute-start | bytes 6291464 | tf_op jit(solution)/shard_map/ppermute | solution.py:86
  242.1 18.1 %all-to-all-start.1 = ((bf16[32,8,512]{2,1,0:T(8,128)(2,1)}), bf16[32,8,512]{2,1,0:T(8,128)(2,1)S(1)}, u32[]{:S(2)}, u32[]{:S(2)}) async-start(bf16[32,8,512]{2,1,0:T(8,128)(2,1)} %convert_element_type.69), calls=%async_computation.1 | async-start | bytes 524288 | tf_op jit(solution)/shard_map/all_to_all | solution.py:81
  260.3 15.2 %all-to-all-start.2 = ((bf16[32,2,1024]{2,1,0:T(2,128)(2,1)}), bf16[32,2,1024]{2,1,0:T(2,128)(2,1)S(1)}, u32[]{:S(2)}, u32[]{:S(2)}) async-start(bf16[32,2,1024]{2,1,0:T(2,128)(2,1)} %reshape.327), calls=%async_computation.2 | async-start | bytes 262144 | tf_op jit(solution)/shard_map/all_to_all | solution.py:142
  276.4 10.0 %copy-start.1 = (pred[256,4352]{0,1:T(8,128)(4,1)S(1)}, pred[256,4352]{0,1:T(8,128)(4,1)}, u32[]{:S(2)}) copy-start(pred[256,4352]{0,1:T(8,128)(4,1)} %compare_and_fusion) | copy-start | bytes 3342340
Sparse Core Ops, SparseCore 0:
  32.9 22.5 all-gather.9
  57.9 88.4 all-gather.5
  153.5 79.0 all-gather.7
where the time goes:
time: 318 us; the launch traced here: 317 us
  waiting for transfers between devices  164 us (52%)
  blocking collectives  60.2 us (19%)
  other arithmetic  37.6 us (12%)
  matrix products  21.2 us (7%)
  between operations  14 us (4%)
  starting transfers between devices  10.9 us (3%)
  local copies, waits for them, and re-layouts  9.22 us (3%)
    all_gather x1, waiting for transfers between devices, local(): lax.all_gather(mine.reshape(count_gy, sub, HD), 'gy', axis=0, tiled=False)  77.7 us
    all_gather x1, waiting for transfers between devices, local(): weights_full = lax.all_gather(stacked, 'gy', axis=1, tiled=True)  67.4 us
    all_gather x1, blocking collectives, local(): gain_full = lax.all_gather(norm_gain, 'gy', axis=0, tiled=True)  36.5 us
    all_to_all x1, blocking collectives, local(): pieces = lax.all_to_all(pieces, 'gy', 1, 1, tiled=True)  23.7 us
    sub x1, other arithmetic, local(): weights = jnp.where(allowed[None], jnp.exp(scores - row_max), 0.0)  18.1 us
    dot_general x1, matrix products, local(): jnp.einsum('qhd,kd->hqk', queries, key_rows, preferred_element_type=jnp.f...  9.99 us
    all_to_all x1, waiting for transfers between devices, local(): lax.all_to_all(queries.reshape(count_gy, sub, query_cols), 'gy', 0, 0, ti...  9.77 us
    all_to_all x1, waiting for transfers between devices, local(): lax.all_to_all(outgoing, 'gy', split_axis=0, concat_axis=0, tiled=True)  9.12 us
  transfers between devices with their start and end apart: 6, of which 4 were waited for; matrix products, arithmetic and copies ran while one was open for 7% of the time, Pallas kernels for 0%

commit v1 on v0

--- a/solution.py
+++ b/solution.py
@@ -55,7 +55,8 @@
     kv_rows = lax.dynamic_slice_in_dim(kv_proj, where_gx * HD, HD, 0)
     stacked = jnp.concatenate([query_proj, kv_rows], axis=0)
     weights_full = lax.all_gather(stacked, "gy", axis=1, tiled=True)
-    gain_full = lax.all_gather(norm_gain, "gy", axis=0, tiled=True)
+    newest = jnp.concatenate([norm_gain for _ in range(lax.axis_size("gy"))], 0)
+    gain_full = lax.all_to_all(newest, axis_name="gy", split_axis=0, concat_axis=0, tiled=True)
     pieces = hidden_in.reshape(blocks_per_slab, count_gy, sub, local_feats)
     pieces = lax.all_to_all(pieces, "gy", 1, 1, tiled=True)
     rows_here = lax.all_gather(pieces, "gx", axis=0, tiled=False)

time: 318 us -> 318 us (level)
  blocking collectives: 60.2 us -> 23.7 us
  waiting for transfers between devices: 164 us -> 195 us
  starting transfers between devices: 10.9 us -> 15.3 us
    all_gather x1 -> x0, blocking collectives: 36.5 us -> none  [local(): gain_full = lax.all_gather(norm_gain, 'gy', axis=0, tiled=True)]
    all_gather x1, waiting for transfers between devices: 67.4 us -> 84.9 us  [local(): weights_full = lax.all_gather(stacked, 'gy', axis=1, tiled=True)]
    all_to_all x0 -> x1, waiting for transfers between devices: none -> 7.99 us  [local(): lax.all_to_all(newest, axis_name='gy', split_axis=0, concat_axis=0, tiled...]
    all_gather x1, waiting for transfers between devices: 0.01 us -> 5.29 us  [local(): rows_here = lax.all_gather(pieces, 'gx', axis=0, tiled=False)]
    all_to_all x0 -> x1, starting transfers between devices: none -> 4.4 us  [local(): lax.all_to_all(newest, axis_name='gy', split_axis=0, concat_axis=0, tiled...]
  transfers between devices with their start and end apart: 6 -> 7, of which waited for: 4 -> 6; matrix products, arithmetic and copies ran while one was open for 7% -> 8% of each run, Pallas kernels for 0% -> 0%
where the time goes in v1:
time: 318 us; the launch traced here: 317 us
  waiting for transfers between devices  195 us (61%)
  other arithmetic  37.6 us (12%)
  blocking collectives  23.7 us (7%)
  matrix products  21.2 us (7%)
  starting transfers between devices  15.3 us (5%)
  between operations  14 us (4%)
  local copies, waits for them, and re-layouts  10.5 us (3%)
    all_gather x1, waiting for transfers between devices, local(): weights_full = lax.all_gather(stacked, 'gy', axis=1, tiled=True)  84.9 us
    all_gather x1, waiting for transfers between devices, local(): lax.all_gather(mine.reshape(count_gy, sub, HD), 'gy', axis=0, tiled=False)  77.7 us
    all_to_all x1, blocking collectives, local(): pieces = lax.all_to_all(pieces, 'gy', 1, 1, tiled=True)  23.7 us
    sub x1, other arithmetic, local(): weights = jnp.where(allowed[None], jnp.exp(scores - row_max), 0.0)  18.1 us
    dot_general x1, matrix products, local(): jnp.einsum('qhd,kd->hqk', queries, key_rows, preferred_element_type=jnp.f...  9.99 us
    all_to_all x1, waiting for transfers between devices, local(): lax.all_to_all(queries.reshape(count_gy, sub, query_cols), 'gy', 0, 0, ti...  9.77 us
    all_to_all x1, waiting for transfers between devices, local(): lax.all_to_all(outgoing, 'gy', split_axis=0, concat_axis=0, tiled=True)  9.12 us
    all_to_all x1, waiting for transfers between devices, local(): lax.all_to_all(newest, axis_name='gy', split_axis=0, concat_axis=0, tiled...  7.99 us
  transfers between devices with their start and end apart: 7, of which 6 were waited for; matrix products, arithmetic and copies ran while one was open for 8% of the time, Pallas kernels for 0%

profile of v1, /device:TPU:2, one launch (start us, length us, event | category | flops | bytes accessed | tf_op | source)
XLA Modules:
  0.0 317.1 jit_solution(10395400145333613642)
XLA Ops:
  7.2 1.0 copy.47
  8.3 23.7 %all_to_all.28 = bf16[4,32,8,128]{3,2,0,1:T(8,128)(2,1)S(1)} all-to-all(bf16[4,32,8,128]{3,2,0,1:T(8,128)(2,1)S(1)} %copy.47), channel_id=1, replica_groups=mesh['gx'=8,'gy'=32] {'gy'}, dimensions={1} | all-to-all | bytes 524288 | tf_op jit(solution)/shard_map/all_to_all | solution.py:61
  32.0 0.7 copy.48
  32.8 1.6 pad_maximum_fusion.1
  34.4 1.3 concatenate.14
  35.7 4.4 %all-to-all-start.1 = ((bf16[32,128,1]{1,2,0:T(2,128)(2,1)}), bf16[32,128,1]{1,2,0:T(2,128)(2,1)S(1)}, u32[]{:S(2)}, u32[]{:S(2)}) async-start(bf16[32,128,1]{1,2,0:T(2,128)(2,1)} %concatenate.14), calls=%async_computation.1 | async-start | bytes 32768 | tf_op jit(solution)/shard_map/all_to_all | solution.py:59
  40.2 0.8 reduce-window.8
  41.1 0.7 bitcast_subtract_fusion
  41.9 8.0 %all-to-all-done.1 = bf16[32,128,1]{1,2,0:T(2,128)(2,1)S(1)} async-done(((bf16[32,128,1]{1,2,0:T(2,128)(2,1)}), bf16[32,128,1]{1,2,0:T(2,128)(2,1)S(1)}, u32[]{:S(2)}, u32[]{:S(2)}) %all-to-all-start.1) | async-done | bytes 8224 | tf_op jit(solution)/shard_map/all_to_all | solution.py:59
  49.9 5.3 %all-gather.9.cloned.1.call-done = bf16[32,32,8,128]{3,2,1,0:T(8,128)(2,1)} async-done(((bf16[4,32,8,128]{3,2,1,0:T(8,128)(2,1)}), bf16[32,32,8,128]{3,2,1,0:T(8,128)(2,1)}) %all-gather.9.cloned.1.call-update) | async-done | bytes 2097168 | tf_op jit(solution)/shard_map/all_gather | solution.py:62
  55.2 2.1 multiply_reduce_fusion
  57.4 4.1 %bitcast_convert_fusion.1 = f32[8,4,32,8,128]{4,3,2,1,0:T(8,128)} fusion(bf16[32,32,8,128]{3,2,1,0:T(8,128)(2,1)} %all-gather.9.cloned.1.call-done), kind=kLoop, calls=%fused_computation.104 | loop fusion | flops 1048576 | bytes 6291456 | tf_op jit(solution)/shard_map/convert_element_type | solution.py:64
  61.5 84.9 %all-gather.5.cloned.1.call-done = bf16[640,4096]{1,0:T(8,128)(2,1)} async-done(((bf16[640,128]{1,0:T(8,128)(2,1)}), bf16[640,4096]{1,0:T(8,128)(2,1)}) %all-gather.5.cloned.1.call-update) | async-done | bytes 5242896 | tf_op jit(solution)/shard_map/all_gather | solution.py:57
  146.4 5.6 %fusion.8 = f32[256,640]{1,0:T(8,128)S(1)} fusion(bf16[640,4096]{1,0:T(8,128)(2,1)} %all-gather.5.cloned.1.call-done, f32[256,4096]{1,0:T(8,128)} %bitcast.63, f32[4096]{0:T(1024)S(1)} %bitcast_convert_fusion, f32[256]{0:T(256)S(1)} %rsqrt.11), kind=kOutput, calls=%fused_computation.15 | convolution fusion | flops 1345323008 | bytes 10109952 | tf_op jit(solution)/shard_map/dot_general | solution.py:72
  152.6 0.7 fusion.43
  153.7 1.2 multiply_cosine_fusion
  155.0 77.7 %all-gather.7.cloned.1.call-done = bf16[32,32,8,128]{3,2,1,0:T(8,128)(2,1)} async-done(((bf16[1,32,8,128]{3,2,1,0:T(8,128)(2,1)}), bf16[32,32,8,128]{3,2,1,0:T(8,128)(2,1)}) %all-gather.7.cloned.1.call-update) | async-done | bytes 2097168 | tf_op jit(solution)/shard_map/all_gather | solution.py:85
  232.6 2.2 copy.50
  234.9 4.4 %compare_and_fusion = pred[256,4352]{0,1:T(8,128)(4,1)} fusion(s32[256]{0:T(256)S(1)} %iota_add_fusion.1, s32[256]{0:T(256)S(1)} %dynamic_slice.26, s32[4352]{0:T(1024)S(1)} %iota_add_fusion, s32[4352]{0:T(1024)S(1)} %dynamic_slice.25), kind=kLoop, calls=%fused_computation.9 | loop fusion | flops 3342336 | bytes 1150976 | tf_op jit(solution)/shard_map/and | solution.py:104
  239.5 1.4 subtract_convert_fusion
  241.3 0.8 convert_element_type.77
  242.1 5.6 %all-to-all-start.2 = ((bf16[32,8,512]{2,1,0:T(8,128)(2,1)}), bf16[32,8,512]{2,1,0:T(8,128)(2,1)S(1)}, u32[]{:S(2)}, u32[]{:S(2)}) async-start(bf16[32,8,512]{2,1,0:T(8,128)(2,1)} %convert_element_type.77), calls=%async_computation.2 | async-start | bytes 524288 | tf_op jit(solution)/shard_map/all_to_all | solution.py:82
  249.1 0.7 reduce.4
  249.8 0.7 reshape.367
  250.5 9.8 %all-to-all-done.2 = bf16[32,8,512]{2,1,0:T(8,128)(2,1)S(1)} async-done(((bf16[32,8,512]{2,1,0:T(8,128)(2,1)}), bf16[32,8,512]{2,1,0:T(8,128)(2,1)S(1)}, u32[]{:S(2)}, u32[]{:S(2)}) %all-to-all-start.2) | async-done | bytes 262176 | tf_op jit(solution)/shard_map/all_to_all | solution.py:82
  260.3 5.1 %all-to-all-start.3 = ((bf16[32,2,1024]{2,1,0:T(2,128)(2,1)}), bf16[32,2,1024]{2,1,0:T(2,128)(2,1)S(1)}, u32[]{:S(2)}, u32[]{:S(2)}) async-start(bf16[32,2,1024]{2,1,0:T(2,128)(2,1)} %reshape.367), calls=%async_computation.3 | async-start | bytes 262144 | tf_op jit(solution)/shard_map/all_to_all | solution.py:143
  265.6 0.8 reshape.355
  266.3 9.1 %all-to-all-done.3 = bf16[32,2,1024]{2,1,0:T(2,128)(2,1)S(1)} async-done(((bf16[32,2,1024]{2,1,0:T(2,128)(2,1)}), bf16[32,2,1024]{2,1,0:T(2,128)(2,1)S(1)}, u32[]{:S(2)}, u32[]{:S(2)}) %all-to-all-start.3) | async-done | bytes 131104 | tf_op jit(solution)/shard_map/all_to_all | solution.py:143
  276.4 10.0 %fusion.22 = f32[4352,256,4]{1,0,2:T(8,128)} fusion(pred[]{:T(512)S(6)} %eq.96, bf16[8192,128]{1,0:T(8,128)(2,1)} %collective-permute-done, s32[]{:T(128)S(6)} %select_n.101, bf16[8192,128]{1,0:T(8,128)(2,1)S(1)} %bitcast.67, bf16[256,4,128]{2,1,0:T(4,128)(2,1)} %reshape.355), kind=kOutput, calls=%fused_computation.23 | convolution fusion | flops 1141407744 | bytes 20316164 | tf_op jit(solution)/shard_map/qhd,kd->hqk/dot_general | solution.py:109
  286.4 18.1 %fusion.60 = (f32[4,256]{1,0:T(4,128)S(1)}, bf16[4,256,4352]{1,2,0:T(8,128)(2,1)}) fusion(f32[4352,256,4]{1,0,2:T(8,128)} %fusion.22, pred[256,4352]{0,1:T(8,128)(4,1)S(1)} %copy-done.1), kind=kOutput, calls=%fused_computation.108 | output fusion | flops 35655936 | bytes 27856896 | tf_op jit(solution)/shard_map/sub | solution.py:114
  304.5 5.3 %fusion.17 = bf16[256,4,128]{0,2,1:T(8,128)(2,1)S(1)} fusion(bf16[4,256,4352]{1,2,0:T(8,128)(2,1)} %get-tuple-element.23, pred[]{:T(512)S(6)} %eq.96, bf16[8192,128]{1,0:T(8,128)(2,1)} %collective-permute-done, s32[]{:T(128)S(6)} %select_n.101, bf16[8192,128]{1,0:T(8,128)(2,1)S(1)} %bitcast.68, f32[256,4]{0,1:T(4,128)S(1)} %bitcast.76), kind=kOutput, calls=%fused_computation.20 | convolution fusion | flops 1141669888 | bytes 11407365 | tf_op jit(solution)/shard_map/hqk,kd->hqd/dot_general | solution.py:116
  309.8 0.8 copy.59
  (51 shorter events, 4.6 us)
Async XLA Ops:
  7.2 25.7 %copy-start = (bf16[1024,128]{1,0:T(8,128)(2,1)S(1)}, bf16[1024,128]{1,0:T(8,128)(2,1)}, u32[]{:S(2)}) copy-start(bf16[1024,128]{1,0:T(8,128)(2,1)} %param.9) | copy-start | bytes 786436
  7.2 48.0 %all-gather.9.cloned.1.call-start = ((), (), s32[]{:S(2)}) async-start(), calls=%async_computation.6 | async-start | bytes 2359296 | tf_op jit(solution)/shard_map/all_gather | solution.py:62
  32.8 113.6 %all-gather.5.cloned.1.call-start = ((), (), s32[]{:S(2)}) async-start(), calls=%async_computation.4 | async-start | bytes 5406720 | tf_op jit(solution)/shard_map/all_gather | solution.py:57
  35.7 14.2 %all-to-all-start.1 = ((bf16[32,128,1]{1,2,0:T(2,128)(2,1)}), bf16[32,128,1]{1,2,0:T(2,128)(2,1)S(1)}, u32[]{:S(2)}, u32[]{:S(2)}) async-start(bf16[32,128,1]{1,2,0:T(2,128)(2,1)} %concatenate.14), calls=%async_computation.1 | async-start | bytes 32768 | tf_op jit(solution)/shard_map/all_to_all | solution.py:59
  40.1 192.5 %all-gather.7.cloned.1.call-start = ((), (), s32[]{:S(2)}) async-start(), calls=%async_computation.5 | async-start | bytes 2162688 | tf_op jit(solution)/shard_map/all_gather | solution.py:85
  146.4 7.3 %copy-start.2 = (s32[512]{0:T(512)S(1)}, s32[512]{0:T(512)}, u32[]{:S(2)}) copy-start(s32[512]{0:T(512)} %param.11) | copy-start | bytes 6148
  234.8 41.6 %collective-permute-start = (bf16[8192,128]{1,0:T(8,128)(2,1)S(1)}, bf16[8192,128]{1,0:T(8,128)(2,1)}, u32[]{:S(2)}, u32[]{:S(2)}) collective-permute-start(bf16[8192,128]{1,0:T(8,128)(2,1)S(1)} %bitcast.65), channel_id=1, source_target_pairs={{0,32},{32,0},{64,96},{96,64},{128,160},{160,128},{192,224},{224,1... | collective-permute-start | bytes 6291464 | tf_op jit(solution)/shard_map/ppermute | solution.py:87
  242.1 18.1 %all-to-all-start.2 = ((bf16[32,8,512]{2,1,0:T(8,128)(2,1)}), bf16[32,8,512]{2,1,0:T(8,128)(2,1)S(1)}, u32[]{:S(2)}, u32[]{:S(2)}) async-start(bf16[32,8,512]{2,1,0:T(8,128)(2,1)} %convert_element_type.77), calls=%async_computation.2 | async-start | bytes 524288 | tf_op jit(solution)/shard_map/all_to_all | solution.py:82
  260.3 15.2 %all-to-all-start.3 = ((bf16[32,2,1024]{2,1,0:T(2,128)(2,1)}), bf16[32,2,1024]{2,1,0:T(2,128)(2,1)S(1)}, u32[]{:S(2)}, u32[]{:S(2)}) async-start(bf16[32,2,1024]{2,1,0:T(2,128)(2,1)} %reshape.367), calls=%async_computation.3 | async-start | bytes 262144 | tf_op jit(solution)/shard_map/all_to_all | solution.py:143
  276.4 10.0 %copy-start.1 = (pred[256,4352]{0,1:T(8,128)(4,1)S(1)}, pred[256,4352]{0,1:T(8,128)(4,1)}, u32[]{:S(2)}) copy-start(pred[256,4352]{0,1:T(8,128)(4,1)} %compare_and_fusion) | copy-start | bytes 3342340
Sparse Core Ops, SparseCore 0:
  32.9 22.2 all-gather.8
  57.6 88.7 all-gather.4
  153.5 79.0 all-gather.6
